TPU v7x, 128 devices: a whole 4x4x4 slice. The times are simulated.
128 devices in a mesh: req: 8 (over x, core), seq: 16 (over z, y).
Axes of the slice: x: 4, y: 4, z: 4, core: 2. Of those that a mesh axis runs over, the one named last changes fastest.
Arguments:
- hidden: bfloat16 [8, 2048, 2048], P('req', 'seq'), may hold values from -6 to 6
- lengths: int32 [8], replicated, may hold values from 1 to 2048, 10240 in all
- slot_request: int32 [8], replicated, may hold values from 0 to 7, each once
- norm_gain: bfloat16 [2048], replicated, may hold values from 0.099609375 to 1.8984375
- in_weight: bfloat16 [2, 2048, 4096], P(None, 'req', 'seq'), may hold values from -0.125 to 0.125
- conv_weight: bfloat16 [4, 4096], P(None, 'seq'), may hold values from -3 to 3
- conv_bias: bfloat16 [4096], P('seq'), may hold values from -0.5 to 0.5
- xproj_weight: bfloat16 [4096, 160], P('seq'), may hold values from -0.09375 to 0.09375
- dt_weight: bfloat16 [128, 4096], P(None, 'seq'), may hold values from -0.5 to 0.5
- dt_bias: bfloat16 [4096], P('seq'), may hold values from -6.91 to -2.25
- a_log: float32 [16, 4096], replicated, may hold values from -2.3 to 1.39
- skip_gain: float32 [4096], replicated, may hold values from 0.5 to 1.5
- out_weight: bfloat16 [4096, 2048], P('seq', 'req'), may hold values from -0.09375 to 0.09375
Outputs:
- mixed: bfloat16 [8, 2048, 2048], P('req', 'seq')
- final_state: float32 [8, 16, 4096], P('req', None, 'seq')
Inputs may be any that keep to these rules, and one draw needn't show every extreme that they name: `lengths`: each slot's length is at least 1, the longest is exactly 2048, and they sum to 10240. `slot_request`: A permutation of the requests.
All inputs are finite; a program needn't handle non-finite values.
Results may differ from a plain program's by a relative error of at most 0.015.
Values may be sent and summed in bfloat16 or wider, within the bound.
No kernel may reach another device: no remote copies, remote signals or barrier semaphores. Data moves between devices by JAX's collectives and lax.ppermute only.
A program may use at most 128 MiB of HBM per device.

v0:
```python
import jax
import jax.numpy as jnp
from jax import lax
from jax.sharding import PartitionSpec as P

STATE = 16
RANK = 128


def gather_a2a(block, axis, dim):
    count = lax.axis_size(axis)
    copies = jnp.broadcast_to(block[None], (count,) + block.shape)
    stacked = lax.all_to_all(copies, axis, split_axis=0, concat_axis=0, tiled=True)
    moved = jnp.moveaxis(stacked, 0, dim)
    shape = list(block.shape)
    shape[dim] = shape[dim] * count
    return moved.reshape(shape)


def to_blocks(array):
    pieces, length, columns = array.shape
    return jnp.moveaxis(array.reshape(pieces, 16, length // 16, columns), 1, 0)


def from_blocks(array):
    count, pieces, group, columns = array.shape
    return jnp.moveaxis(array, 0, 1).reshape(pieces, count * group, columns)


def piece_scan(rates, values, entry, readout, decay):
    pieces, length, columns = rates.shape
    group = length // 16
    positions = jnp.arange(length, dtype=jnp.int32)
    lower = (positions[None, :] <= positions[:, None]).astype(jnp.float32)
    running = jnp.einsum("rs,psw->prw", lower, rates, precision=lax.Precision.HIGHEST)

    def advance(state, items):
        rate, value, into, outof = items
        outputs = []
        for place in range(group):
            factor = jnp.exp(rate[:, place][:, None, :] * decay[None])
            state = (
                factor * state
                + (rate[:, place] * value[:, place])[:, None, :] * into[:, place][:, :, None]
            )
            outputs.append(jnp.sum(outof[:, place][:, :, None] * state, axis=1))
        return (state, jnp.stack(outputs, axis=1))

    start = jnp.zeros((pieces, decay.shape[0], columns), jnp.float32)
    end_local, local_out = lax.scan(
        advance, start, (to_blocks(rates), to_blocks(values), to_blocks(entry), to_blocks(readout))
    )
    total_decay = jnp.exp(running[:, length - 1][:, None, :] * decay[None])
    return (end_local, from_blocks(local_out), total_decay, running)


def carried_part(running, readout, decay, carry_in):

    def correct(items):
        total, outof = items
        kept = jnp.exp(total[:, :, None, :] * decay[None, None]) * carry_in[:, None]
        return jnp.sum(outof[:, :, :, None] * kept, axis=2)

    return from_blocks(lax.map(correct, (to_blocks(running), to_blocks(readout))))


def per_device(
    hidden,
    lengths,
    slot_request,
    norm_gain,
    in_weight,
    conv_weight,
    conv_bias,
    xproj_weight,
    dt_weight,
    dt_bias,
    a_log,
    skip_gain,
    out_weight,
):
    seq_count = lax.axis_size("seq")
    seq_index = lax.axis_index("seq")
    req_index = lax.axis_index("req")
    rows = hidden.shape[1]
    span = rows * seq_count
    width = in_weight.shape[2]
    taps_count = conv_weight.shape[0]
    state_count = a_log.shape[0]
    tokens = hidden[0].astype(jnp.float32)
    scale = lax.rsqrt(jnp.mean(tokens * tokens, axis=-1, keepdims=True) + 1e-05)
    normed = (tokens * scale * norm_gain.astype(jnp.float32)).astype(jnp.bfloat16)
    w_in = gather_a2a(in_weight, "req", 1)
    w_flat = jnp.concatenate((w_in[0], w_in[1]), axis=1)
    both = jnp.dot(
        lax.all_gather(normed, "seq", axis=0, tiled=True),
        w_flat,
        preferred_element_type=jnp.float32,
    )
    xin = both[:, :width]
    zgate = both[:, width:].astype(jnp.bfloat16)
    padded = jnp.pad(xin, ((taps_count - 1, 0), (0, 0)))
    taps = conv_weight.astype(jnp.float32)
    convolved = conv_bias.astype(jnp.float32) + jnp.zeros_like(xin)
    for tap in range(taps_count):
        convolved = convolved + taps[tap] * padded[tap : tap + span, :]
    inner = jax.nn.silu(convolved).astype(jnp.bfloat16)
    inner_tok = lax.all_to_all(inner, "seq", split_axis=0, concat_axis=1, tiled=True)
    xproj_full = gather_a2a(xproj_weight, "seq", 0)
    dt_full = gather_a2a(dt_weight, "seq", 1)
    dt_bias_full = gather_a2a(dt_bias, "seq", 0)
    proj = jnp.dot(inner_tok, xproj_full, preferred_element_type=jnp.float32)
    length_here = lax.dynamic_index_in_dim(lengths, req_index, 0, keepdims=False)
    positions = seq_index * rows + jnp.arange(rows, dtype=jnp.int32)
    live = (positions < length_here).astype(jnp.float32)
    rate_low = proj[:, :RANK].astype(jnp.bfloat16)
    delta_tok = (
        jax.nn.softplus(
            jnp.dot(rate_low, dt_full, preferred_element_type=jnp.float32)
            + dt_bias_full.astype(jnp.float32)
        )
        * live[:, None]
    )
    w_out = gather_a2a(out_weight, "req", 1)
    decay = -jnp.exp(a_log)
    inner_f = inner_tok.astype(jnp.float32)
    entry = proj[None, :, RANK : RANK + STATE]
    readout = proj[None, :, RANK + STATE :]
    end_local, local_out, total_decay, running = piece_scan(
        delta_tok[None], inner_f[None], entry, readout, decay
    )
    pair = jnp.stack((total_decay[0], end_local[0])).reshape(2, state_count, seq_count, width)
    pair_ch = lax.all_to_all(pair, "seq", split_axis=2, concat_axis=2, tiled=True)
    carry = jnp.zeros((state_count, width), jnp.float32)
    carries = []
    for block in range(seq_count):
        carries.append(carry)
        carry = pair_ch[0, :, block] * carry + pair_ch[1, :, block]
    carry_ch = jnp.stack(carries, axis=1)
    carry_in = lax.all_to_all(carry_ch, "seq", split_axis=1, concat_axis=1, tiled=True).reshape(
        state_count, seq_count * width
    )
    carried = carried_part(running, readout, decay, carry_in[None])
    scanned = ((local_out + carried)[0] + skip_gain * inner_f).astype(jnp.bfloat16)
    scanned_ch = lax.all_to_all(scanned, "seq", split_axis=1, concat_axis=0, tiled=True)
    gated_ch = (scanned_ch.astype(jnp.float32) * jax.nn.silu(zgate.astype(jnp.float32))).astype(
        jnp.bfloat16
    )
    branch = lax.psum_scatter(
        jnp.dot(gated_ch, w_out, preferred_element_type=jnp.float32).astype(jnp.bfloat16),
        "seq",
        scatter_dimension=0,
        tiled=True,
    ).astype(jnp.float32)
    slot_all = gather_a2a(carry[None], "req", 0)
    picked = (slot_request == req_index).astype(jnp.float32)
    final_state = jnp.sum(picked[:, None, None] * slot_all, axis=0, keepdims=True)
    mixed = (tokens + branch).astype(jnp.bfloat16)[None]
    return (mixed, final_state)


def solution(mesh):
    in_specs = (
        P("req", "seq", None),
        P(),
        P(),
        P(),
        P(None, "req", "seq"),
        P(None, "seq"),
        P("seq"),
        P("seq", None),
        P(None, "seq"),
        P("seq"),
        P(),
        P(),
        P("seq", "req"),
    )
    out_specs = (P("req", "seq", None), P("req", None, "seq"))
    return jax.shard_map(
        per_device, mesh=mesh, in_specs=in_specs, out_specs=out_specs, check_vma=False
    )
```

profile of v0, /device:TPU:0, one launch (start us, length us, event | category | flops | bytes accessed | tf_op | source)
XLA Modules:
  0.0 439.4 jit_solution(5524272800325330019)
XLA Ops:
  12.9 4.5 %all-to-all-start = ((bf16[8,2,256,256]{3,2,1,0:T(8,128)(2,1)}), bf16[8,2,256,256]{3,2,1,0:T(8,128)(2,1)S(1)}, u32[]{:S(2)}, u32[]{:S(2)}) async-start(bf16[8,2,256,256]{3,2,1,0:T(8,128)(2,1)} %broadcast_in_dim.25), calls=%async_computation | async-start | bytes 4194304 | tf_op jit(solution)/shard_map/all_to_all | solution.py:13
  19.3 25.3 %all-to-all-done = bf16[8,2,256,256]{3,2,1,0:T(8,128)(2,1)S(1)} async-done(((bf16[8,2,256,256]{3,2,1,0:T(8,128)(2,1)}), bf16[8,2,256,256]{3,2,1,0:T(8,128)(2,1)S(1)}, u32[]{:S(2)}, u32[]{:S(2)}) %all-to-all-start) | async-done | bytes 2097184 | tf_op jit(solution)/shard_map/all_to_all | solution.py:13
  44.6 8.0 %all-to-all-start.4 = ((bf16[16,2,128]{2,1,0:T(2,128)(2,1)}), bf16[16,2,128]{2,1,0:T(2,128)(2,1)S(1)}, u32[]{:S(2)}, u32[]{:S(2)}) async-start(bf16[16,2,128]{2,1,0:T(2,128)(2,1)} %reshape.2341), calls=%async_computation.4 | async-start | bytes 16384 | tf_op jit(solution)/shard_map/all_to_all | solution.py:13
  54.1 6.2 %all-to-all-done.4 = bf16[16,2,128]{2,1,0:T(2,128)(2,1)S(1)} async-done(((bf16[16,2,128]{2,1,0:T(2,128)(2,1)}), bf16[16,2,128]{2,1,0:T(2,128)(2,1)S(1)}, u32[]{:S(2)}, u32[]{:S(2)}) %all-to-all-start.4) | async-done | bytes 8224 | tf_op jit(solution)/shard_map/all_to_all | solution.py:13
  61.5 3.7 all-to-all-start.2
  65.2 33.5 %all-gather.2.cloned.1.call-done = bf16[2048,2048]{1,0:T(8,128)(2,1)} async-done(((bf16[128,2048]{1,0:T(8,128)(2,1)}), bf16[2048,2048]{1,0:T(8,128)(2,1)}) %all-gather.2.cloned.1.call-update) | async-done | bytes 8388624 | tf_op jit(solution)/shard_map/all_gather | solution.py:96
  98.7 7.2 %fusion.29 = f32[2048,512]{1,0:T(8,128)S(1)} fusion(bf16[2048,2048]{1,0:T(8,128)(2,1)} %all-gather.2.cloned.1.call-done, bf16[2048,256]{1,0:T(8,128)(2,1)} %bitcast.737, bf16[2048,256]{1,0:T(8,128)(2,1)S(1)} %bitcast.736), kind=kOutput, calls=%fused_computation.84 | convolution fusion | flops 4299161600 | bytes 14680064 | tf_op jit(solution)/shard_map/dot_general | solution.py:95
  110.2 5.5 %all-to-all-start.1 = ((bf16[16,128,256]{2,1,0:T(8,128)(2,1)}), bf16[16,128,256]{2,1,0:T(8,128)(2,1)S(1)}, u32[]{:S(2)}, u32[]{:S(2)}) async-start(bf16[16,128,256]{2,1,0:T(8,128)(2,1)} %bitcast.691), calls=%async_computation.1 | async-start | bytes 2097152 | tf_op jit(solution)/shard_map/all_to_all | solution.py:108
  115.9 17.4 %all-to-all-done.1 = bf16[16,128,256]{2,1,0:T(8,128)(2,1)S(1)} async-done(((bf16[16,128,256]{2,1,0:T(8,128)(2,1)}), bf16[16,128,256]{2,1,0:T(8,128)(2,1)S(1)}, u32[]{:S(2)}, u32[]{:S(2)}) %all-to-all-start.1) | async-done | bytes 1048608 | tf_op jit(solution)/shard_map/all_to_all | solution.py:108
  134.4 4.5 %all-to-all-start.3 = ((bf16[16,128,256]{1,2,0:T(8,128)(2,1)}), bf16[16,128,256]{1,2,0:T(8,128)(2,1)}, u32[]{:S(2)}, u32[]{:S(2)}) async-start(bf16[16,128,256]{1,2,0:T(8,128)(2,1)} %broadcast_in_dim.27), calls=%async_computation.3 | async-start | bytes 2097152 | tf_op jit(solution)/shard_map/all_to_all | solution.py:13
  140.8 13.7 %all-to-all-done.3 = bf16[16,128,256]{1,2,0:T(8,128)(2,1)} async-done(((bf16[16,128,256]{1,2,0:T(8,128)(2,1)}), bf16[16,128,256]{1,2,0:T(8,128)(2,1)}, u32[]{:S(2)}, u32[]{:S(2)}) %all-to-all-start.3) | async-done | bytes 1048608 | tf_op jit(solution)/shard_map/all_to_all | solution.py:13
  167.5 55.2 %while.24 = (s32[]{:T(128)}, f32[1,16,4096]{2,1,0:T(8,128)S(1)}, f32[16,1,8,4096]{3,2,1,0:T(8,128)}, f32[16,1,8,4096]{3,2,1,0:T(8,128)}, f32[16,4096]{1,0:T(8,12...) while((s32[]{:T(128)}, f32[1,16,4096]{2,1,0:T(8,128)S(1)}, ...), condition=%wide.region_10.11_spmd.clone, body=%wide.region_1.10_spmd.clone.sunk | while | flops 4849667 | bytes 4347896 | solution.py:50
  224.0 3.6 all-to-all-start.5
  228.2 9.5 %all-to-all-done.5 = f32[2,16,16,256]{3,1,0,2:T(8,128)S(1)} async-done(((f32[2,16,16,256]{3,1,0,2:T(8,128)}), f32[2,16,16,256]{3,1,0,2:T(8,128)S(1)}, u32[]{:S(2)}, u32[]{:S(2)}) %all-to-all-start.5) | async-done | bytes 524320 | tf_op jit(solution)/shard_map/all_to_all | solution.py:133
  246.8 3.5 all-to-all-start.6
  250.4 8.6 %all-to-all-done.6 = f32[16,16,256]{2,0,1:T(8,128)S(1)} async-done(((f32[16,16,256]{2,0,1:T(8,128)}), f32[16,16,256]{2,0,1:T(8,128)S(1)}, u32[]{:S(2)}, u32[]{:S(2)}) %all-to-all-start.6) | async-done | bytes 262176 | tf_op jit(solution)/shard_map/all_to_all | solution.py:140
  260.8 38.5 %while.23 = (s32[]{:T(128)}, f32[16,1,8,4096]{3,2,1,0:T(8,128)}, f32[16,1,8,16]{3,2,1,0:T(8,128)S(1)}, f32[16,1,8,4096]{3,2,1,0:T(8,128)}, f32[16,4096]{1,0:T(8,128)S(1)}, /*index=5*/f32[16,16,256]{2,1,0:T(8,128)S(1)}, s32[]{:T(128)}) while((s32[]{:T(128)}, f32[16,1,8,4096]{3,2,1,0:T(8,128)}, f32[16,1,8,16]{3,2,1,0:T(8,128)S(1)}, ...), condition=%wide.region_13.14_spmd, body=%wide.region_11.13_spmd.sunk | while | flops 2064386 | bytes 1837141 | solution.py:64
  304.7 4.0 all-to-all-start.7
  308.8 12.8 %all-to-all-done.7 = bf16[128,16,256]{2,0,1:T(8,128)(2,1)S(1)} async-done(((bf16[128,16,256]{2,0,1:T(8,128)(2,1)}), bf16[128,16,256]{2,0,1:T(8,128)(2,1)S(1)}, u32[]{:S(2)}, u32[]{:S(2)}) %all-to-all-start.7) | async-done | bytes 1048608 | tf_op jit(solution)/shard_map/all_to_all | solution.py:145
  322.7 4.3 all-to-all-start.8
  329.3 13.6 %all-to-all-done.8 = bf16[8,256,256]{1,2,0:T(8,128)(2,1)S(1)} async-done(((bf16[8,256,256]{1,2,0:T(8,128)(2,1)}), bf16[8,256,256]{1,2,0:T(8,128)(2,1)S(1)}, u32[]{:S(2)}, u32[]{:S(2)}) %all-to-all-start.8) | async-done | bytes 1048608 | tf_op jit(solution)/shard_map/all_to_all | solution.py:13
  342.9 5.6 %convolution_convert_fusion = bf16[2048,2048]{1,0:T(8,128)(2,1)} fusion(bf16[2048,256]{1,0:T(8,128)(2,1)S(1)} %fusion.36, bf16[256,2048]{0,1:T(8,128)(2,1)S(1)} %bitcast.692), kind=kOutput, calls=%fused_computation.73 | convolution fusion | flops 2151677952 | bytes 10485760 | tf_op jit(solution)/shard_map/dot_general | solution.py:150
  352.7 6.0 %all-to-all-done.9 = f32[8,1,16,256]{3,2,1,0:T(8,128)S(1)} async-done(((f32[8,1,16,256]{3,2,1,0:T(8,128)}), f32[8,1,16,256]{3,2,1,0:T(8,128)S(1)}, u32[]{:S(2)}, u32[]{:S(2)}) %all-to-all-start.9) | async-done | bytes 131104 | tf_op jit(solution)/shard_map/all_to_all | solution.py:13
  359.3 71.3 %reduce-scatter.2.cloned.1.call-done = bf16[128,2048]{1,0:T(8,128)(2,1)} async-done(((bf16[2048,2048]{1,0:T(8,128)(2,1)}), bf16[128,2048]{1,0:T(8,128)(2,1)}) %reduce-scatter.2.cloned.1.call-update) | async-done | bytes 524304 | tf_op jit(solution)/shard_map/reduce_scatter | solution.py:149
  (362 shorter events, 151.1 us)
Async XLA Ops:
  7.2 4.1 copy-start.5
  7.2 91.6 %all-gather.2.cloned.1.call-start = ((), (), s32[]{:S(2)}) async-start(), calls=%async_computation.11 | async-start | bytes 8912896 | tf_op jit(solution)/shard_map/all_gather | solution.py:96
  12.9 4.6 %copy-start.13 = (bf16[256]{0:T(256)(128)(2,1)S(1)}, bf16[256]{0:T(256)(128)(2,1)}, u32[]{:S(2)}) copy-start(bf16[256]{0:T(256)(128)(2,1)} %param.23) | copy-start | bytes 1540
  12.9 4.6 %copy-start.12 = (bf16[256]{0:T(256)(128)(2,1)S(1)}, bf16[256]{0:T(256)(128)(2,1)}, u32[]{:S(2)}) copy-start(bf16[256]{0:T(256)(128)(2,1)} %param.26) | copy-start | bytes 1540
  12.9 6.4 %copy-start.11 = (bf16[4,256]{1,0:T(4,128)(2,1)S(1)}, bf16[4,256]{1,0:T(4,128)(2,1)}, u32[]{:S(2)}) copy-start(bf16[4,256]{1,0:T(4,128)(2,1)} %param.22) | copy-start | bytes 6148
  12.9 31.7 %all-to-all-start = ((bf16[8,2,256,256]{3,2,1,0:T(8,128)(2,1)}), bf16[8,2,256,256]{3,2,1,0:T(8,128)(2,1)S(1)}, u32[]{:S(2)}, u32[]{:S(2)}) async-start(bf16[8,2,256,256]{3,2,1,0:T(8,128)(2,1)} %broadcast_in_dim.25), calls=%async_computation | async-start | bytes 4194304 | tf_op jit(solution)/shard_map/all_to_all | solution.py:13
  44.6 15.7 %all-to-all-start.4 = ((bf16[16,2,128]{2,1,0:T(2,128)(2,1)}), bf16[16,2,128]{2,1,0:T(2,128)(2,1)S(1)}, u32[]{:S(2)}, u32[]{:S(2)}) async-start(bf16[16,2,128]{2,1,0:T(2,128)(2,1)} %reshape.2341), calls=%async_computation.4 | async-start | bytes 16384 | tf_op jit(solution)/shard_map/all_to_all | solution.py:13
  52.6 7.6 %copy-start.8 = (bf16[256,160]{0,1:T(8,128)(2,1)S(1)}, bf16[256,160]{0,1:T(8,128)(2,1)}, u32[]{:S(2)}) copy-start(bf16[256,160]{0,1:T(8,128)(2,1)} %param.24) | copy-start | bytes 245764
  54.1 44.7 %copy-start.4 = (bf16[1,8,256,256]{3,2,0,1:T(8,128)(2,1)S(1)}, bf16[1,8,256,256]{3,2,0,1:T(8,128)(2,1)}, u32[]{:S(2)}) copy-start(bf16[1,8,256,256]{3,2,0,1:T(8,128)(2,1)} %get-tuple-element.265) | copy-start | bytes 3145732
  61.5 48.7 %all-to-all-start.2 = ((bf16[16,256,160]{1,2,0:T(8,128)(2,1)}), bf16[16,256,160]{1,2,0:T(8,128)(2,1)S(1)}, u32[]{:S(2)}, u32[]{:S(2)}) async-start(bf16[16,256,160]{1,2,0:T(8,128)(2,1)} %broadcast_in_dim.26), calls=%async_computation.2 | async-start | bytes 2621440 | tf_op jit(solution)/shard_map/all_to_all | solution.py:13
  107.9 7.9 %copy-start.9 = (bf16[128,256]{1,0:T(8,128)(2,1)S(1)}, bf16[128,256]{1,0:T(8,128)(2,1)}, u32[]{:S(2)}) copy-start(bf16[128,256]{1,0:T(8,128)(2,1)} %param.25) | copy-start | bytes 196612
  110.2 23.0 %all-to-all-start.1 = ((bf16[16,128,256]{2,1,0:T(8,128)(2,1)}), bf16[16,128,256]{2,1,0:T(8,128)(2,1)S(1)}, u32[]{:S(2)}, u32[]{:S(2)}) async-start(bf16[16,128,256]{2,1,0:T(8,128)(2,1)} %bitcast.691), calls=%async_computation.1 | async-start | bytes 2097152 | tf_op jit(solution)/shard_map/all_to_all | solution.py:108
  115.7 23.2 %copy-start.14 = (s32[8]{0:T(128)S(1)}, s32[8]{0:T(128)}, u32[]{:S(2)}) copy-start(s32[8]{0:T(128)} %param.18) | copy-start | bytes 100
  134.4 20.1 %all-to-all-start.3 = ((bf16[16,128,256]{1,2,0:T(8,128)(2,1)}), bf16[16,128,256]{1,2,0:T(8,128)(2,1)}, u32[]{:S(2)}, u32[]{:S(2)}) async-start(bf16[16,128,256]{1,2,0:T(8,128)(2,1)} %broadcast_in_dim.27), calls=%async_computation.3 | async-start | bytes 2097152 | tf_op jit(solution)/shard_map/all_to_all | solution.py:13
  222.9 27.5 %copy-start.10 = (f32[4096]{0:T(1024)S(1)}, f32[4096]{0:T(1024)}, u32[]{:S(2)}) copy-start(f32[4096]{0:T(1024)} %param.28) | copy-start | bytes 49156
  224.0 13.7 %all-to-all-start.5 = ((f32[2,16,16,256]{3,1,0,2:T(8,128)}), f32[2,16,16,256]{3,1,0,2:T(8,128)S(1)}, u32[]{:S(2)}, u32[]{:S(2)}) async-start(f32[2,16,16,256]{3,1,0,2:T(8,128)} %copy.165), calls=%async_computation.5 | async-start | bytes 1048576 | tf_op jit(solution)/shard_map/all_to_all | solution.py:133
  246.8 12.2 %all-to-all-start.6 = ((f32[16,16,256]{2,0,1:T(8,128)}), f32[16,16,256]{2,0,1:T(8,128)S(1)}, u32[]{:S(2)}, u32[]{:S(2)}) async-start(f32[16,16,256]{2,0,1:T(8,128)} %constant_dynamic-update-slice_fusion), calls=%async_computation.6 | async-start | bytes 524288 | tf_op jit(solution)/shard_map/all_to_all | solution.py:140
  304.7 4.0 copy-start.7
  304.7 16.9 %all-to-all-start.7 = ((bf16[128,16,256]{2,0,1:T(8,128)(2,1)}), bf16[128,16,256]{2,0,1:T(8,128)(2,1)S(1)}, u32[]{:S(2)}, u32[]{:S(2)}) async-start(bf16[128,16,256]{2,0,1:T(8,128)(2,1)} %fusion.33), calls=%async_computation.7 | async-start | bytes 2097152 | tf_op jit(solution)/shard_map/all_to_all | solution.py:145
  322.7 20.2 %all-to-all-start.8 = ((bf16[8,256,256]{1,2,0:T(8,128)(2,1)}), bf16[8,256,256]{1,2,0:T(8,128)(2,1)S(1)}, u32[]{:S(2)}, u32[]{:S(2)}) async-start(bf16[8,256,256]{1,2,0:T(8,128)(2,1)} %broadcast_in_dim.29), calls=%async_computation.8 | async-start | bytes 2097152 | tf_op jit(solution)/shard_map/all_to_all | solution.py:13
  327.0 103.6 %reduce-scatter.2.cloned.1.call-start = ((), (), s32[]{:S(2)}) async-start(), calls=%async_computation.12 | async-start | bytes 8912896 | tf_op jit(solution)/shard_map/reduce_scatter | solution.py:149
  348.6 4.1 copy-start.15
  348.6 82.1 %copy-start = (bf16[1,128,2048]{2,1,0:T(8,128)(2,1)S(1)}, bf16[1,128,2048]{2,1,0:T(8,128)(2,1)}, u32[]{:S(2)}) copy-start(bf16[1,128,2048]{2,1,0:T(8,128)(2,1)} %param.17) | copy-start | bytes 1572868
  349.2 9.4 %all-to-all-start.9 = ((f32[8,1,16,256]{3,2,1,0:T(8,128)}), f32[8,1,16,256]{3,2,1,0:T(8,128)S(1)}, u32[]{:S(2)}, u32[]{:S(2)}) async-start(f32[8,1,16,256]{3,2,1,0:T(8,128)} %broadcast_in_dim.31), calls=%async_computation.10 | async-start | bytes 262144 | tf_op jit(solution)/shard_map/all_to_all | solution.py:13
  (4 other events, 7.5 us)
Sparse Core Ops, SparseCore 0:
  11.4 87.3 all-gather.1
  348.7 81.8 reduce-scatter.1
where the time goes:
time: 441 us; the launch traced here: 439 us
  waiting for transfers between devices  218 us (49%)
  local copies, waits for them, and re-layouts  83.7 us (19%)
  other arithmetic  59.4 us (13%)
  starting transfers between devices  45.1 us (10%)
  matrix products  17.2 us (4%)
  between operations  14.4 us (3%)
    reduce_scatter x1, waiting for transfers between devices, per_device(): lax.psum_scatter(jnp.dot(gated_ch, w_out, preferred_element_type=jnp.floa...  71.3 us
    all_to_all x6, waiting for transfers between devices, gather_a2a(): lax.all_to_all(copies, axis, split_axis=0, concat_axis=0, tiled=True)  64.8 us
    all_gather x1, waiting for transfers between devices, per_device(): lax.all_gather(normed, 'seq', axis=0, tiled=True)  33.5 us
    all_to_all x6, starting transfers between devices, gather_a2a(): lax.all_to_all(copies, axis, split_axis=0, concat_axis=0, tiled=True)  28.4 us
    dynamic_update_slice x32, local copies, waits for them, and re-layouts, piece_scan(): lax.scan(advance, start, (to_blocks(rates), to_blocks(values), to_blocks(...  21.3 us
    reduce_sum x48, other arithmetic, advance(): outputs.append(jnp.sum(outof[:, place][:, :, None] * state, axis=1))  19.8 us
    all_to_all x1, waiting for transfers between devices, per_device(): lax.all_to_all(inner, 'seq', split_axis=0, concat_axis=1, tiled=True)  17.4 us
    squeeze x32, local copies, waits for them, and re-layouts, piece_scan(): lax.scan(advance, start, (to_blocks(rates), to_blocks(values), to_blocks(...  15.9 us
  transfers between devices with their start and end apart: 12, of which 11 were waited for; matrix products, arithmetic and copies ran while one was open for 5% of the time, Pallas kernels for 0%

commit v1 on v0

--- a/solution.py
+++ b/solution.py
@@ -5,6 +5,22 @@
 
 STATE = 16
 RANK = 128
+
+
+def collect(x, axis, dim):
+    ways, here, step = (lax.axis_size(axis), lax.axis_index(axis), x.shape[dim])
+    lengths = [n * ways if d == dim else n for d, n in enumerate(x.shape)]
+    full = lax.dynamic_update_slice_in_dim(jnp.zeros(lengths, x.dtype), x, here * step, axis=dim)
+    going_up = going_down = x
+    for far in range(1, ways // 2 + 1):
+        going_up = lax.ppermute(going_up, axis, [(d, (d + 1) % ways) for d in range(ways)])
+        full = lax.dynamic_update_slice_in_dim(full, going_up, (here - far) % ways * step, axis=dim)
+        if 2 * far < ways:
+            going_down = lax.ppermute(going_down, axis, [(d, (d - 1) % ways) for d in range(ways)])
+            full = lax.dynamic_update_slice_in_dim(
+                full, going_down, (here + far) % ways * step, axis=dim
+            )
+    return full
 
 
 def gather_a2a(block, axis, dim):
@@ -92,11 +108,7 @@
     normed = (tokens * scale * norm_gain.astype(jnp.float32)).astype(jnp.bfloat16)
     w_in = gather_a2a(in_weight, "req", 1)
     w_flat = jnp.concatenate((w_in[0], w_in[1]), axis=1)
-    both = jnp.dot(
-        lax.all_gather(normed, "seq", axis=0, tiled=True),
-        w_flat,
-        preferred_element_type=jnp.float32,
-    )
+    both = jnp.dot(collect(normed, "seq", 0), w_flat, preferred_element_type=jnp.float32)
     xin = both[:, :width]
     zgate = both[:, width:].astype(jnp.bfloat16)
     padded = jnp.pad(xin, ((taps_count - 1, 0), (0, 0)))

time: 441 us -> 492 us (1.12)
  starting transfers between devices: 45.1 us -> 81.6 us
  local copies, waits for them, and re-layouts: 83.7 us -> 110 us
  waiting for transfers between devices: 218 us -> 205 us
    ppermute x0 -> x15, waiting for transfers between devices: none -> 53.1 us  [the longest x8 32.2 us: collect(): lax.ppermute(going_up, axis, [(d, (d + 1) % ways) for d in range(ways)])]
    ppermute x0 -> x15, starting transfers between devices: none -> 39.8 us  [the longest x7 38.1 us: collect(): lax.ppermute(going_down, axis, [(d, (d - 1) % ways) for d in range(ways)])]
    all_gather x1 -> x0, waiting for transfers between devices: 33.5 us -> none  [per_device(): lax.all_gather(normed, 'seq', axis=0, tiled=True)]
    all_to_all x6, waiting for transfers between devices: 64.8 us -> 36.7 us  [gather_a2a(): lax.all_to_all(copies, axis, split_axis=0, concat_axis=0, tiled=True)]
    dynamic_update_slice x0 -> x15, local copies, waits for them, and re-layouts: none -> 21.2 us  [the longest x8 12.1 us: collect(): lax.dynamic_update_slice_in_dim(full, going_up, (here - far) % ways * ste...]
  transfers between devices with their start and end apart: 12 -> 26, of which waited for: 11 -> 18; matrix products, arithmetic and copies ran while one was open for 5% -> 9% of each run, Pallas kernels for 0% -> 0%
where the time goes in v1:
time: 492 us; the launch traced here: 490 us
  waiting for transfers between devices  205 us (42%)
  local copies, waits for them, and re-layouts  110 us (22%)
  starting transfers between devices  81.6 us (17%)
  other arithmetic  58.4 us (12%)
  matrix products  18.5 us (4%)
  between operations  14.5 us (3%)
    reduce_scatter x1, waiting for transfers between devices, per_device(): lax.psum_scatter(jnp.dot(gated_ch, w_out, preferred_element_type=jnp.floa...  71 us
    ppermute x7, starting transfers between devices, collect(): lax.ppermute(going_down, axis, [(d, (d - 1) % ways) for d in range(ways)])  38.1 us
    all_to_all x6, waiting for transfers between devices, gather_a2a(): lax.all_to_all(copies, axis, split_axis=0, concat_axis=0, tiled=True)  36.7 us
    ppermute x8, waiting for transfers between devices, collect(): lax.ppermute(going_up, axis, [(d, (d + 1) % ways) for d in range(ways)])  32.2 us
    all_to_all x6, starting transfers between devices, gather_a2a(): lax.all_to_all(copies, axis, split_axis=0, concat_axis=0, tiled=True)  27 us
    dynamic_update_slice x32, local copies, waits for them, and re-layouts, piece_scan(): lax.scan(advance, start, (to_blocks(rates), to_blocks(values), to_blocks(...  21.5 us
    ppermute x7, waiting for transfers between devices, collect(): lax.ppermute(going_down, axis, [(d, (d - 1) % ways) for d in range(ways)])  20.9 us
    reduce_sum x48, other arithmetic, advance(): outputs.append(jnp.sum(outof[:, place][:, :, None] * state, axis=1))  19.8 us
  transfers between devices with their start and end apart: 26, of which 18 were waited for; matrix products, arithmetic and copies ran while one was open for 9% of the time, Pallas kernels for 0%

profile of v1, /device:TPU:0, one launch (start us, length us, event | category | flops | bytes accessed | tf_op | source)
XLA Modules:
  0.0 489.9 jit_solution(9225230851471426846)
XLA Ops:
  16.2 4.9 %collective-permute-start.1 = (bf16[128,2048]{1,0:T(8,128)(2,1)S(1)}, bf16[128,2048]{1,0:T(8,128)(2,1)}, u32[]{:S(2)}, u32[]{:S(2)}) collective-permute-start(bf16[128,2048]{1,0:T(8,128)(2,1)S(1)} %get-tuple-element.230), channel_id=1, source_target_pairs={{0,15},{1,0},{2,1},{3,2},{4,3},{5,4},{6,5},{7,6},{8,7},{9,8},{10,9... | collective-permute-start | bytes 1572872 | tf_op jit(solution)/shard_map/ppermute | solution.py:19
  21.1 11.9 %collective-permute-done = bf16[128,2048]{1,0:T(8,128)(2,1)S(1)} collective-permute-done((bf16[128,2048]{1,0:T(8,128)(2,1)S(1)}, bf16[128,2048]{1,0:T(8,128)(2,1)S(1)}, u32[]{:S(2)}, u32[]{:S(2)}) %collective-permute-start) | collective-permute-done | bytes 524320 | tf_op jit(solution)/shard_map/ppermute | solution.py:16
  38.4 11.2 %collective-permute-done.2 = bf16[128,2048]{1,0:T(8,128)(2,1)} collective-permute-done((bf16[128,2048]{1,0:T(8,128)(2,1)S(1)}, bf16[128,2048]{1,0:T(8,128)(2,1)}, u32[]{:S(2)}, u32[]{:S(2)}) %collective-permute-start.2) | collective-permute-done | bytes 524320 | tf_op jit(solution)/shard_map/ppermute | solution.py:16
  57.4 5.4 %collective-permute-start.5 = (bf16[128,2048]{1,0:T(8,128)(2,1)S(1)}, bf16[128,2048]{1,0:T(8,128)(2,1)S(1)}, u32[]{:S(2)}, u32[]{:S(2)}) collective-permute-start(bf16[128,2048]{1,0:T(8,128)(2,1)S(1)} %collective-permute-done.3), channel_id=1, source_target_pairs={{0,15},{1,0},{2,1},{3,2},{4,3},{5,4},{6,5},{7,6},{8,7},{9,8},{10,9... | collective-permute-start | bytes 1572872 | tf_op jit(solution)/shard_map/ppermute | solution.py:19
  74.7 5.8 %collective-permute-start.7 = (bf16[128,2048]{1,0:T(8,128)(2,1)S(1)}, bf16[128,2048]{1,0:T(8,128)(2,1)}, u32[]{:S(2)}, u32[]{:S(2)}) collective-permute-start(bf16[128,2048]{1,0:T(8,128)(2,1)S(1)} %collective-permute-done.5), channel_id=1, source_target_pairs={{0,15},{1,0},{2,1},{3,2},{4,3},{5,4},{6,5},{7,6},{8,7},{9,8},{10,9... | collective-permute-start | bytes 1572872 | tf_op jit(solution)/shard_map/ppermute | solution.py:19
  84.1 7.4 %collective-permute-done.7 = bf16[128,2048]{1,0:T(8,128)(2,1)} collective-permute-done((bf16[128,2048]{1,0:T(8,128)(2,1)S(1)}, bf16[128,2048]{1,0:T(8,128)(2,1)}, u32[]{:S(2)}, u32[]{:S(2)}) %collective-permute-start.7) | collective-permute-done | bytes 524320 | tf_op jit(solution)/shard_map/ppermute | solution.py:19
  91.5 5.9 %collective-permute-start.9 = (bf16[128,2048]{1,0:T(8,128)(2,1)}, bf16[128,2048]{1,0:T(8,128)(2,1)}, u32[]{:S(2)}, u32[]{:S(2)}) collective-permute-start(bf16[128,2048]{1,0:T(8,128)(2,1)} %collective-permute-done.7), channel_id=1, source_target_pairs={{0,15},{1,0},{2,1},{3,2},{4,3},{5,4},{6,5},{7,6},{8,7},{9,8},{10,9... | collective-permute-start | bytes 1572872 | tf_op jit(solution)/shard_map/ppermute | solution.py:19
  97.4 6.7 %all-to-all-start.4 = ((bf16[16,2,128]{2,1,0:T(2,128)(2,1)}), bf16[16,2,128]{2,1,0:T(2,128)(2,1)S(1)}, u32[]{:S(2)}, u32[]{:S(2)}) async-start(bf16[16,2,128]{2,1,0:T(2,128)(2,1)} %reshape.2341), calls=%async_computation.4 | async-start | bytes 16384 | tf_op jit(solution)/shard_map/all_to_all | solution.py:29
  107.9 5.8 %collective-permute-start.11 = (bf16[128,2048]{1,0:T(8,128)(2,1)}, bf16[128,2048]{1,0:T(8,128)(2,1)S(1)}, u32[]{:S(2)}, u32[]{:S(2)}) collective-permute-start(bf16[128,2048]{1,0:T(8,128)(2,1)} %collective-permute-done.9), channel_id=1, source_target_pairs={{0,15},{1,0},{2,1},{3,2},{4,3},{5,4},{6,5},{7,6},{8,7},{9,8},{10,9... | collective-permute-start | bytes 1572872 | tf_op jit(solution)/shard_map/ppermute | solution.py:19
  123.2 5.7 %collective-permute-start.13 = (bf16[128,2048]{1,0:T(8,128)(2,1)S(1)}, bf16[128,2048]{1,0:T(8,128)(2,1)S(1)}, u32[]{:S(2)}, u32[]{:S(2)}) collective-permute-start(bf16[128,2048]{1,0:T(8,128)(2,1)S(1)} %collective-permute-done.11), channel_id=1, source_target_pairs={{0,15},{1,0},{2,1},{3,2},{4,3},{5,4},{6,5},{7,6},{8,7},{9,8},{10,9... | collective-permute-start | bytes 1572872 | tf_op jit(solution)/shard_map/ppermute | solution.py:19
  138.1 6.6 %collective-permute-done.14 = bf16[128,2048]{1,0:T(8,128)(2,1)S(1)} collective-permute-done((bf16[128,2048]{1,0:T(8,128)(2,1)S(1)}, bf16[128,2048]{1,0:T(8,128)(2,1)S(1)}, u32[]{:S(2)}, u32[]{:S(2)}) %collective-permute-start.14) | collective-permute-done | bytes 524320 | tf_op jit(solution)/shard_map/ppermute | solution.py:16
  150.6 7.2 %fusion.29 = f32[2048,512]{1,0:T(8,128)S(1)} fusion(bf16[2048,2048]{1,0:T(8,128)(2,1)} %constant_dynamic-update-slice_fusion.16, bf16[2048,256]{1,0:T(8,128)(2,1)} %bitcast.737, bf16[2048,256]{1,0:T(8,128)(2,1)S(1)} %bitcast.736), kind=kOutput, calls=%fused_computation.84 | convolution fusion | flops 4299161600 | bytes 14680064 | tf_op jit(solution)/shard_map/dot_general | solution.py:111
  162.1 5.6 %all-to-all-done.2 = bf16[16,256,160]{1,2,0:T(8,128)(2,1)S(1)} async-done(((bf16[16,256,160]{1,2,0:T(8,128)(2,1)}), bf16[16,256,160]{1,2,0:T(8,128)(2,1)S(1)}, u32[]{:S(2)}, u32[]{:S(2)}) %all-to-all-start.2) | async-done | bytes 1310752 | tf_op jit(solution)/shard_map/all_to_all | solution.py:29
  171.5 13.2 %all-to-all-done.1 = bf16[16,128,256]{2,1,0:T(8,128)(2,1)S(1)} async-done(((bf16[16,128,256]{2,1,0:T(8,128)(2,1)}), bf16[16,128,256]{2,1,0:T(8,128)(2,1)S(1)}, u32[]{:S(2)}, u32[]{:S(2)}) %all-to-all-start.1) | async-done | bytes 1048608 | tf_op jit(solution)/shard_map/all_to_all | solution.py:120
  192.0 11.5 %all-to-all-done.3 = bf16[16,128,256]{1,2,0:T(8,128)(2,1)} async-done(((bf16[16,128,256]{1,2,0:T(8,128)(2,1)}), bf16[16,128,256]{1,2,0:T(8,128)(2,1)}, u32[]{:S(2)}, u32[]{:S(2)}) %all-to-all-start.3) | async-done | bytes 1048608 | tf_op jit(solution)/shard_map/all_to_all | solution.py:29
  216.6 55.3 %while.24 = (s32[]{:T(128)}, f32[1,16,4096]{2,1,0:T(8,128)S(1)}, f32[16,1,8,4096]{3,2,1,0:T(8,128)}, f32[16,1,8,4096]{3,2,1,0:T(8,128)}, f32[16,4096]{1,0:T(8,12...) while((s32[]{:T(128)}, f32[1,16,4096]{2,1,0:T(8,128)S(1)}, ...), condition=%wide.region_10.11_spmd.clone, body=%wide.region_1.10_spmd.clone.sunk | while | flops 4849667 | bytes 4347896 | solution.py:66
  277.7 9.3 %all-to-all-done.5 = f32[2,16,16,256]{3,1,0,2:T(8,128)S(1)} async-done(((f32[2,16,16,256]{3,1,0,2:T(8,128)}), f32[2,16,16,256]{3,1,0,2:T(8,128)S(1)}, u32[]{:S(2)}, u32[]{:S(2)}) %all-to-all-start.5) | async-done | bytes 524320 | tf_op jit(solution)/shard_map/all_to_all | solution.py:145
  299.6 8.6 %all-to-all-done.6 = f32[16,16,256]{2,0,1:T(8,128)S(1)} async-done(((f32[16,16,256]{2,0,1:T(8,128)}), f32[16,16,256]{2,0,1:T(8,128)S(1)}, u32[]{:S(2)}, u32[]{:S(2)}) %all-to-all-start.6) | async-done | bytes 262176 | tf_op jit(solution)/shard_map/all_to_all | solution.py:152
  310.0 38.5 %while.23 = (s32[]{:T(128)}, f32[16,1,8,4096]{3,2,1,0:T(8,128)}, f32[16,1,8,16]{3,2,1,0:T(8,128)S(1)}, f32[16,1,8,4096]{3,2,1,0:T(8,128)}, f32[16,4096]{1,0:T(8,128)S(1)}, /*index=5*/f32[16,16,256]{2,1,0:T(8,128)S(1)}, s32[]{:T(128)}) while((s32[]{:T(128)}, f32[16,1,8,4096]{3,2,1,0:T(8,128)}, f32[16,1,8,16]{3,2,1,0:T(8,128)S(1)}, ...), condition=%wide.region_13.14_spmd, body=%wide.region_11.13_spmd.sunk | while | flops 2064386 | bytes 1837141 | solution.py:80
  358.0 13.2 %all-to-all-done.7 = bf16[128,16,256]{2,0,1:T(8,128)(2,1)S(1)} async-done(((bf16[128,16,256]{2,0,1:T(8,128)(2,1)}), bf16[128,16,256]{2,0,1:T(8,128)(2,1)S(1)}, u32[]{:S(2)}, u32[]{:S(2)}) %all-to-all-start.7) | async-done | bytes 1048608 | tf_op jit(solution)/shard_map/all_to_all | solution.py:157
  378.8 13.6 %all-to-all-done.8 = bf16[8,256,256]{1,2,0:T(8,128)(2,1)} async-done(((bf16[8,256,256]{1,2,0:T(8,128)(2,1)}), bf16[8,256,256]{1,2,0:T(8,128)(2,1)}, u32[]{:S(2)}, u32[]{:S(2)}) %all-to-all-start.8) | async-done | bytes 1048608 | tf_op jit(solution)/shard_map/all_to_all | solution.py:29
  392.4 6.9 %convolution_convert_fusion = bf16[2048,2048]{1,0:T(8,128)(2,1)} fusion(bf16[2048,256]{1,0:T(8,128)(2,1)S(1)} %fusion.36, bf16[256,2048]{0,1:T(8,128)(2,1)} %bitcast.65), kind=kOutput, calls=%fused_computation.73 | convolution fusion | flops 2151677952 | bytes 10485760 | tf_op jit(solution)/shard_map/dot_general | solution.py:162
  403.4 6.0 %all-to-all-done.9 = f32[8,1,16,256]{3,2,1,0:T(8,128)S(1)} async-done(((f32[8,1,16,256]{3,2,1,0:T(8,128)}), f32[8,1,16,256]{3,2,1,0:T(8,128)S(1)}, u32[]{:S(2)}, u32[]{:S(2)}) %all-to-all-start.9) | async-done | bytes 131104 | tf_op jit(solution)/shard_map/all_to_all | solution.py:29
  410.1 71.0 %reduce-scatter.2.cloned.1.call-done = bf16[128,2048]{1,0:T(8,128)(2,1)} async-done(((bf16[2048,2048]{1,0:T(8,128)(2,1)}), bf16[128,2048]{1,0:T(8,128)(2,1)}) %reduce-scatter.2.cloned.1.call-update) | async-done | bytes 524304 | tf_op jit(solution)/shard_map/reduce_scatter | solution.py:161
  (411 shorter events, 230.6 us)
Async XLA Ops:
  14.4 18.6 %collective-permute-start = (bf16[128,2048]{1,0:T(8,128)(2,1)S(1)}, bf16[128,2048]{1,0:T(8,128)(2,1)S(1)}, u32[]{:S(2)}, u32[]{:S(2)}) collective-permute-start(bf16[128,2048]{1,0:T(8,128)(2,1)S(1)} %get-tuple-element.230), channel_id=1, source_target_pairs={{0,1},{1,2},{2,3},{3,4},{4,5},{5,6},{6,7},{7,8},{8,9},{9,10},{10,1... | collective-permute-start | bytes 1572872 | tf_op jit(solution)/shard_map/ppermute | solution.py:16
  16.2 17.6 %collective-permute-start.1 = (bf16[128,2048]{1,0:T(8,128)(2,1)S(1)}, bf16[128,2048]{1,0:T(8,128)(2,1)}, u32[]{:S(2)}, u32[]{:S(2)}) collective-permute-start(bf16[128,2048]{1,0:T(8,128)(2,1)S(1)} %get-tuple-element.230), channel_id=1, source_target_pairs={{0,15},{1,0},{2,1},{3,2},{4,3},{5,4},{6,5},{7,6},{8,7},{9,8},{10,9... | collective-permute-start | bytes 1572872 | tf_op jit(solution)/shard_map/ppermute | solution.py:19
  33.0 16.5 %collective-permute-start.2 = (bf16[128,2048]{1,0:T(8,128)(2,1)S(1)}, bf16[128,2048]{1,0:T(8,128)(2,1)}, u32[]{:S(2)}, u32[]{:S(2)}) collective-permute-start(bf16[128,2048]{1,0:T(8,128)(2,1)S(1)} %collective-permute-done), channel_id=1, source_target_pairs={{0,1},{1,2},{2,3},{3,4},{4,5},{5,6},{6,7},{7,8},{8,9},{9,10},{10,1... | collective-permute-start | bytes 1572872 | tf_op jit(solution)/shard_map/ppermute | solution.py:16
  33.8 23.6 %collective-permute-start.3 = (bf16[128,2048]{1,0:T(8,128)(2,1)}, bf16[128,2048]{1,0:T(8,128)(2,1)S(1)}, u32[]{:S(2)}, u32[]{:S(2)}) collective-permute-start(bf16[128,2048]{1,0:T(8,128)(2,1)} %collective-permute-done.1), channel_id=1, source_target_pairs={{0,15},{1,0},{2,1},{3,2},{4,3},{5,4},{6,5},{7,6},{8,7},{9,8},{10,9... | collective-permute-start | bytes 1572872 | tf_op jit(solution)/shard_map/ppermute | solution.py:19
  49.5 15.9 %collective-permute-start.4 = (bf16[128,2048]{1,0:T(8,128)(2,1)}, bf16[128,2048]{1,0:T(8,128)(2,1)}, u32[]{:S(2)}, u32[]{:S(2)}) collective-permute-start(bf16[128,2048]{1,0:T(8,128)(2,1)} %collective-permute-done.2), channel_id=1, source_target_pairs={{0,1},{1,2},{2,3},{3,4},{4,5},{5,6},{6,7},{7,8},{8,9},{9,10},{10,1... | collective-permute-start | bytes 1572872 | tf_op jit(solution)/shard_map/ppermute | solution.py:16
  51.1 46.3 %all-to-all-start = ((bf16[8,2,256,256]{3,2,1,0:T(8,128)(2,1)}), bf16[8,2,256,256]{3,2,1,0:T(8,128)(2,1)S(1)}, u32[]{:S(2)}, u32[]{:S(2)}) async-start(bf16[8,2,256,256]{3,2,1,0:T(8,128)(2,1)} %broadcast_in_dim.28), calls=%async_computation | async-start | bytes 4194304 | tf_op jit(solution)/shard_map/all_to_all | solution.py:29
  57.4 17.3 %collective-permute-start.5 = (bf16[128,2048]{1,0:T(8,128)(2,1)S(1)}, bf16[128,2048]{1,0:T(8,128)(2,1)S(1)}, u32[]{:S(2)}, u32[]{:S(2)}) collective-permute-start(bf16[128,2048]{1,0:T(8,128)(2,1)S(1)} %collective-permute-done.3), channel_id=1, source_target_pairs={{0,15},{1,0},{2,1},{3,2},{4,3},{5,4},{6,5},{7,6},{8,7},{9,8},{10,9... | collective-permute-start | bytes 1572872 | tf_op jit(solution)/shard_map/ppermute | solution.py:19
  65.4 15.1 %collective-permute-start.6 = (bf16[128,2048]{1,0:T(8,128)(2,1)}, bf16[128,2048]{1,0:T(8,128)(2,1)S(1)}, u32[]{:S(2)}, u32[]{:S(2)}) collective-permute-start(bf16[128,2048]{1,0:T(8,128)(2,1)} %collective-permute-done.4), channel_id=1, source_target_pairs={{0,1},{1,2},{2,3},{3,4},{4,5},{5,6},{6,7},{7,8},{8,9},{9,10},{10,1... | collective-permute-start | bytes 1572872 | tf_op jit(solution)/shard_map/ppermute | solution.py:16
  74.7 16.8 %collective-permute-start.7 = (bf16[128,2048]{1,0:T(8,128)(2,1)S(1)}, bf16[128,2048]{1,0:T(8,128)(2,1)}, u32[]{:S(2)}, u32[]{:S(2)}) collective-permute-start(bf16[128,2048]{1,0:T(8,128)(2,1)S(1)} %collective-permute-done.5), channel_id=1, source_target_pairs={{0,15},{1,0},{2,1},{3,2},{4,3},{5,4},{6,5},{7,6},{8,7},{9,8},{10,9... | collective-permute-start | bytes 1572872 | tf_op jit(solution)/shard_map/ppermute | solution.py:19
  80.5 16.9 %collective-permute-start.8 = (bf16[128,2048]{1,0:T(8,128)(2,1)S(1)}, bf16[128,2048]{1,0:T(8,128)(2,1)}, u32[]{:S(2)}, u32[]{:S(2)}) collective-permute-start(bf16[128,2048]{1,0:T(8,128)(2,1)S(1)} %collective-permute-done.6), channel_id=1, source_target_pairs={{0,1},{1,2},{2,3},{3,4},{4,5},{5,6},{6,7},{7,8},{8,9},{9,10},{10,1... | collective-permute-start | bytes 1572872 | tf_op jit(solution)/shard_map/ppermute | solution.py:16
  91.5 16.5 %collective-permute-start.9 = (bf16[128,2048]{1,0:T(8,128)(2,1)}, bf16[128,2048]{1,0:T(8,128)(2,1)}, u32[]{:S(2)}, u32[]{:S(2)}) collective-permute-start(bf16[128,2048]{1,0:T(8,128)(2,1)} %collective-permute-done.7), channel_id=1, source_target_pairs={{0,15},{1,0},{2,1},{3,2},{4,3},{5,4},{6,5},{7,6},{8,7},{9,8},{10,9... | collective-permute-start | bytes 1572872 | tf_op jit(solution)/shard_map/ppermute | solution.py:19
  97.4 18.2 %collective-permute-start.10 = (bf16[128,2048]{1,0:T(8,128)(2,1)}, bf16[128,2048]{1,0:T(8,128)(2,1)}, u32[]{:S(2)}, u32[]{:S(2)}) collective-permute-start(bf16[128,2048]{1,0:T(8,128)(2,1)} %collective-permute-done.8), channel_id=1, source_target_pairs={{0,1},{1,2},{2,3},{3,4},{4,5},{5,6},{6,7},{7,8},{8,9},{9,10},{10,1... | collective-permute-start | bytes 1572872 | tf_op jit(solution)/shard_map/ppermute | solution.py:16
  97.4 48.1 %all-to-all-start.4 = ((bf16[16,2,128]{2,1,0:T(2,128)(2,1)}), bf16[16,2,128]{2,1,0:T(2,128)(2,1)S(1)}, u32[]{:S(2)}, u32[]{:S(2)}) async-start(bf16[16,2,128]{2,1,0:T(2,128)(2,1)} %reshape.2341), calls=%async_computation.4 | async-start | bytes 16384 | tf_op jit(solution)/shard_map/all_to_all | solution.py:29
  107.9 15.3 %collective-permute-start.11 = (bf16[128,2048]{1,0:T(8,128)(2,1)}, bf16[128,2048]{1,0:T(8,128)(2,1)S(1)}, u32[]{:S(2)}, u32[]{:S(2)}) collective-permute-start(bf16[128,2048]{1,0:T(8,128)(2,1)} %collective-permute-done.9), channel_id=1, source_target_pairs={{0,15},{1,0},{2,1},{3,2},{4,3},{5,4},{6,5},{7,6},{8,7},{9,8},{10,9... | collective-permute-start | bytes 1572872 | tf_op jit(solution)/shard_map/ppermute | solution.py:19
  115.6 15.2 %collective-permute-start.12 = (bf16[128,2048]{1,0:T(8,128)(2,1)}, bf16[128,2048]{1,0:T(8,128)(2,1)S(1)}, u32[]{:S(2)}, u32[]{:S(2)}) collective-permute-start(bf16[128,2048]{1,0:T(8,128)(2,1)} %collective-permute-done.10), channel_id=1, source_target_pairs={{0,1},{1,2},{2,3},{3,4},{4,5},{5,6},{6,7},{7,8},{8,9},{9,10},{10,1... | collective-permute-start | bytes 1572872 | tf_op jit(solution)/shard_map/ppermute | solution.py:16
  123.2 14.1 %collective-permute-start.13 = (bf16[128,2048]{1,0:T(8,128)(2,1)S(1)}, bf16[128,2048]{1,0:T(8,128)(2,1)S(1)}, u32[]{:S(2)}, u32[]{:S(2)}) collective-permute-start(bf16[128,2048]{1,0:T(8,128)(2,1)S(1)} %collective-permute-done.11), channel_id=1, source_target_pairs={{0,15},{1,0},{2,1},{3,2},{4,3},{5,4},{6,5},{7,6},{8,7},{9,8},{10,9... | collective-permute-start | bytes 1572872 | tf_op jit(solution)/shard_map/ppermute | solution.py:19
  130.8 13.9 %collective-permute-start.14 = (bf16[128,2048]{1,0:T(8,128)(2,1)S(1)}, bf16[128,2048]{1,0:T(8,128)(2,1)S(1)}, u32[]{:S(2)}, u32[]{:S(2)}) collective-permute-start(bf16[128,2048]{1,0:T(8,128)(2,1)S(1)} %collective-permute-done.12), channel_id=1, source_target_pairs={{0,1},{1,2},{2,3},{3,4},{4,5},{5,6},{6,7},{7,8},{8,9},{9,10},{10,1... | collective-permute-start | bytes 1572872 | tf_op jit(solution)/shard_map/ppermute | solution.py:16
  146.7 21.0 %all-to-all-start.2 = ((bf16[16,256,160]{1,2,0:T(8,128)(2,1)}), bf16[16,256,160]{1,2,0:T(8,128)(2,1)S(1)}, u32[]{:S(2)}, u32[]{:S(2)}) async-start(bf16[16,256,160]{1,2,0:T(8,128)(2,1)} %broadcast_in_dim.29), calls=%async_computation.2 | async-start | bytes 2621440 | tf_op jit(solution)/shard_map/all_to_all | solution.py:29
  167.7 17.0 %all-to-all-start.1 = ((bf16[16,128,256]{2,1,0:T(8,128)(2,1)}), bf16[16,128,256]{2,1,0:T(8,128)(2,1)S(1)}, u32[]{:S(2)}, u32[]{:S(2)}) async-start(bf16[16,128,256]{2,1,0:T(8,128)(2,1)} %bitcast.692), calls=%async_computation.1 | async-start | bytes 2097152 | tf_op jit(solution)/shard_map/all_to_all | solution.py:120
  185.9 17.7 %all-to-all-start.3 = ((bf16[16,128,256]{1,2,0:T(8,128)(2,1)}), bf16[16,128,256]{1,2,0:T(8,128)(2,1)}, u32[]{:S(2)}, u32[]{:S(2)}) async-start(bf16[16,128,256]{1,2,0:T(8,128)(2,1)} %broadcast_in_dim.30), calls=%async_computation.3 | async-start | bytes 2097152 | tf_op jit(solution)/shard_map/all_to_all | solution.py:29
  273.3 13.7 %all-to-all-start.5 = ((f32[2,16,16,256]{3,1,0,2:T(8,128)}), f32[2,16,16,256]{3,1,0,2:T(8,128)S(1)}, u32[]{:S(2)}, u32[]{:S(2)}) async-start(f32[2,16,16,256]{3,1,0,2:T(8,128)} %copy.165), calls=%async_computation.5 | async-start | bytes 1048576 | tf_op jit(solution)/shard_map/all_to_all | solution.py:145
  354.0 17.1 %all-to-all-start.7 = ((bf16[128,16,256]{2,0,1:T(8,128)(2,1)}), bf16[128,16,256]{2,0,1:T(8,128)(2,1)S(1)}, u32[]{:S(2)}, u32[]{:S(2)}) async-start(bf16[128,16,256]{2,0,1:T(8,128)(2,1)} %fusion.33), calls=%async_computation.7 | async-start | bytes 2097152 | tf_op jit(solution)/shard_map/all_to_all | solution.py:157
  372.2 20.2 %all-to-all-start.8 = ((bf16[8,256,256]{1,2,0:T(8,128)(2,1)}), bf16[8,256,256]{1,2,0:T(8,128)(2,1)}, u32[]{:S(2)}, u32[]{:S(2)}) async-start(bf16[8,256,256]{1,2,0:T(8,128)(2,1)} %broadcast_in_dim.32), calls=%async_computation.8 | async-start | bytes 2097152 | tf_op jit(solution)/shard_map/all_to_all | solution.py:29
  376.5 104.6 %reduce-scatter.2.cloned.1.call-start = ((), (), s32[]{:S(2)}) async-start(), calls=%async_computation.11 | async-start | bytes 8912896 | tf_op jit(solution)/shard_map/reduce_scatter | solution.py:161
  (21 other events, 194.2 us)
Sparse Core Ops, SparseCore 0:
  399.5 81.5 reduce-scatter.1
